TPU v7x, 32 devices: a whole 2x2x4 slice. The times are simulated.
32 devices in a mesh: grp: 4 (over x, core), tp: 8 (over z, y).
Axes of the slice: x: 2, y: 2, z: 4, core: 2. Of those that a mesh axis runs over, the one named last changes fastest.
Arguments:
- hidden_in: bfloat16 [3072, 3584], P('grp'), may hold values from -6 to 6
- lengths: int32 [8, 8], P('grp'), may hold values from 1 to 96, 384 in all within a row
- dest: int32 [64, 1], P('grp'), may hold values from 0 to 3; in each aligned block of 16 rows (0 to 15, 16 to 31, ...) at most 4 rows name the same one
- attn_gain: float32 [3584], replicated, may hold values from 0.6 to 8
- q_weight: bfloat16 [3584, 2048], P('grp', 'tp'), may hold values from -0.09375 to 0.09375
- k_weight: bfloat16 [3584, 512], P('grp', 'tp'), may hold values from -0.09375 to 0.09375
- v_weight: bfloat16 [3584, 512], P('grp', 'tp'), may hold values from -0.09375 to 0.09375
- o_weight: bfloat16 [3584, 2048], P('grp', 'tp'), may hold values from -0.125 to 0.125
- ffn_gain: float32 [3584], replicated, may hold values from 0.1 to 1.9
- gate_weight: bfloat16 [3584, 10240], P('grp', 'tp'), may hold values from -0.09375 to 0.09375
- up_weight: bfloat16 [3584, 10240], P('grp', 'tp'), may hold values from -0.09375 to 0.09375
- down_weight: bfloat16 [3584, 10240], P('grp', 'tp'), may hold values from -0.0625 to 0.0625
Outputs:
- bank_in: bfloat16 [4, 4, 4, 3584], P('grp', None, None, 'tp')
Inputs may be any that keep to these rules, and one draw needn't show every extreme that they name: Each block's 8 lengths sum to 384. `dest`: among the programs of one index of grp, no bank shard is named by more than 4.
All inputs are finite; a program needn't handle non-finite values.
Results may differ from a plain program's by a relative error of at most 0.015.
The roundings to bfloat16 on the way count: a program that leaves them out, or rounds other values in their place, can miss the bound.
Values may be sent and summed in bfloat16 or wider, within the bound.
No kernel may reach another device: no remote copies, remote signals or barrier semaphores. Data moves between devices by JAX's collectives and lax.ppermute only.
A program may use at most 128 MiB of HBM per device.

v0:
```python
import jax
import jax.numpy as jnp
from jax import lax
from jax.sharding import PartitionSpec as P

HEAD_SIZE = 128
KVH = 4
HEADS = 16
EPSILON = 1e-06
HIGH = lax.Precision.HIGHEST


def rms_scale(rows, gain):
    rows = rows.astype(jnp.float32)
    factor = lax.rsqrt(jnp.mean(rows * rows, axis=1, keepdims=True) + EPSILON)
    return (rows * factor * gain[None, :]).astype(jnp.bfloat16)


def segment_ids(lengths, block_rows):
    bounds = jnp.cumsum(lengths, axis=1)
    position = lax.broadcasted_iota(jnp.int32, (lengths.shape[0], block_rows), 1)
    return jnp.sum((position[:, :, None] >= bounds[:, None, :]).astype(jnp.int32), axis=2)


def softmax_rows(attention_scores):
    top = jnp.max(attention_scores, axis=-1, keepdims=True)
    expo = jnp.exp(attention_scores - top)
    return (expo / jnp.sum(expo, axis=-1, keepdims=True)).astype(jnp.bfloat16)


def transposed_dot(left, right):
    return lax.dot_general(
        left, right, (((1,), (1,)), ((), ())), preferred_element_type=jnp.float32
    )


def on_device(
    hidden_in,
    lengths,
    dest,
    attn_gain,
    q_weight,
    k_weight,
    v_weight,
    o_weight,
    ffn_gain,
    gate_weight,
    up_weight,
    down_weight,
):
    row_count, width = hidden_in.shape
    blocks, per_block = lengths.shape
    block_rows = row_count // blocks
    programs = blocks * per_block
    tp_size = lax.axis_size("tp")
    grp_size = lax.axis_size("grp")
    local_heads = q_weight.shape[1] // HEAD_SIZE
    norm_in = rms_scale(hidden_in, attn_gain)
    q_full, k_full, v_full, o_full, gate_full, up_full, down_full = (
        lax.all_gather(q_weight, "grp", axis=0, tiled=True),
        lax.all_gather(k_weight, "grp", axis=0, tiled=True),
        lax.all_gather(v_weight, "grp", axis=0, tiled=True),
        lax.all_gather(o_weight, "grp", axis=0, tiled=True),
        lax.all_gather(gate_weight, "grp", axis=0, tiled=True),
        lax.all_gather(up_weight, "grp", axis=0, tiled=True),
        lax.all_gather(down_weight, "grp", axis=0, tiled=True),
    )
    queries = jnp.dot(norm_in, q_full, preferred_element_type=jnp.float32).astype(jnp.bfloat16)
    key_part = jnp.dot(norm_in, k_full, preferred_element_type=jnp.float32).astype(jnp.bfloat16)
    value_part = jnp.dot(norm_in, v_full, preferred_element_type=jnp.float32).astype(jnp.bfloat16)
    keys_all, vals_all = (
        lax.all_gather(key_part, "tp", axis=1, tiled=True),
        lax.all_gather(value_part, "tp", axis=1, tiled=True),
    )
    kv_count = keys_all.shape[1] // HEAD_SIZE
    kv_index = lax.axis_index("tp") * local_heads // (HEADS // KVH)
    key_head = lax.dynamic_slice_in_dim(
        keys_all.reshape(row_count, HEAD_SIZE, kv_count), kv_index, 1, 2
    )[:, :, 0]
    value_head = lax.dynamic_slice_in_dim(
        vals_all.reshape(row_count, HEAD_SIZE, kv_count), kv_index, 1, 2
    )[:, :, 0]
    segs = segment_ids(lengths, block_rows)
    same = segs[:, :, None] == segs[:, None, :]
    blocked_queries = queries.reshape(blocks, block_rows, local_heads, HEAD_SIZE)
    blocked_keys = key_head.reshape(blocks, block_rows, HEAD_SIZE)
    blocked_values = value_head.reshape(blocks, block_rows, HEAD_SIZE)
    attention_scores = jnp.einsum(
        "xwre,xpe->xrwp", blocked_queries, blocked_keys, preferred_element_type=jnp.float32
    ) * HEAD_SIZE ** (-0.5)
    attention_scores = jnp.where(same[:, None, :, :], attention_scores, -1e30)
    attention_probabilities = softmax_rows(attention_scores)
    attended_rows = jnp.einsum(
        "asfo,aon->afsn",
        attention_probabilities,
        blocked_values,
        preferred_element_type=jnp.float32,
    )
    attended_rows = attended_rows.astype(jnp.bfloat16).reshape(row_count, local_heads * HEAD_SIZE)
    attn_term = transposed_dot(attended_rows, o_full)
    attn_total = lax.psum(attn_term.astype(jnp.bfloat16), "tp").astype(jnp.float32)
    residual = hidden_in.astype(jnp.float32) + attn_total
    norm_mid = rms_scale(residual, ffn_gain)
    gate_pre = jnp.dot(norm_mid, gate_full, preferred_element_type=jnp.float32)
    up_pre = jnp.dot(norm_mid, up_full, preferred_element_type=jnp.float32)
    hidden_ffn = (jax.nn.silu(gate_pre) * up_pre).astype(jnp.bfloat16)
    ffn_term = transposed_dot(hidden_ffn, down_full)
    share = row_count // tp_size
    tp_index = lax.axis_index("tp")
    block_index = lax.broadcasted_iota(jnp.int32, (blocks, block_rows), 0)
    program_of_row = (block_index * per_block + segs).reshape(row_count)
    program_grid = lax.broadcasted_iota(jnp.int32, (programs, row_count), 0)
    selector = program_grid == program_of_row[None, :]
    selector_float = selector.astype(jnp.float32)
    residual_share = lax.dynamic_slice_in_dim(residual, tp_index * share, share, 0)
    selector_share = lax.dynamic_slice_in_dim(selector_float, tp_index * share, share, 1)
    ffn_share = lax.psum_scatter(
        ffn_term.astype(jnp.bfloat16), "tp", scatter_dimension=0, tiled=True
    ).astype(jnp.float32)
    pooled_part = jnp.dot(
        selector_share,
        residual_share + ffn_share,
        precision=HIGH,
        preferred_element_type=jnp.float32,
    )
    pooled_sums = lax.psum_scatter(
        pooled_part.astype(jnp.bfloat16), "tp", scatter_dimension=1, tiled=True
    ).astype(jnp.float32)
    counts = lengths.reshape(programs).astype(jnp.float32)
    embedded = (pooled_sums / counts[:, None]).astype(jnp.bfloat16)
    capacity = max(2, (programs + grp_size - 1) // grp_size)
    targets = dest[:, 0]
    grp_ids = lax.broadcasted_iota(jnp.int32, (programs, grp_size), 1)
    chosen = (targets[:, None] == grp_ids).astype(jnp.int32)
    earlier = jnp.cumsum(chosen, axis=0) - chosen
    slot_rank = jnp.sum(earlier * chosen, axis=1)
    slot_ids = targets * capacity + slot_rank
    slot_grid = lax.broadcasted_iota(jnp.int32, (grp_size * capacity, programs), 0)
    placer = (slot_grid == slot_ids[None, :]).astype(jnp.bfloat16)
    outgoing = jnp.dot(placer, embedded, preferred_element_type=jnp.float32).astype(jnp.bfloat16)
    outgoing = outgoing.reshape(grp_size, capacity, embedded.shape[1])
    incoming = lax.all_to_all(outgoing, "grp", split_axis=0, concat_axis=0, tiled=True)
    return incoming.reshape(1, grp_size, capacity, embedded.shape[1])


def solution(mesh):
    placed = (
        P("grp", None),
        P("grp", None),
        P("grp", None),
        P(),
        P("grp", "tp"),
        P("grp", "tp"),
        P("grp", "tp"),
        P("grp", "tp"),
        P(),
        P("grp", "tp"),
        P("grp", "tp"),
        P("grp", "tp"),
    )
    return jax.shard_map(
        on_device, mesh=mesh, in_specs=placed, out_specs=P("grp", None, None, "tp"), check_vma=False
    )
```

profile of v0, /device:TPU:0, one launch (start us, length us, event | category | flops | bytes accessed | tf_op | source)
XLA Modules:
  0.0 716.7 jit_solution(17084657934199434864)
XLA Ops:
  6.5 0.7 all-gather.6.cloned.1.call-update
  7.3 0.0 all-gather.8.cloned.1.call-start
  7.3 0.7 all-gather.8.cloned.1.call-update
  8.0 0.0 all-reduce.2.cloned.1.call-start
  8.1 0.0 copy-start
  8.1 3.9 fusion.1
  11.9 8.3 %all_gather.27 = bf16[3584,64]{0,1:T(8,128)(2,1)S(1)} all-gather(bf16[896,64]{0,1:T(8,128)(2,1)S(1)} %copy-done.2), channel_id=1, replica_groups=mesh['grp'=4,'tp'=8] {'grp'}, dimensions={0}, use_global_device_ids=true | all-gather | bytes 573440 | tf_op jit(solution)/shard_map/all_gather | solution.py:62
  20.2 2.2 fusion.3
  22.4 2.4 copy-done.1
  24.8 1.8 convolution_convert_fusion.6
  26.6 32.6 %all_gather.28 = bf16[768,512]{0,1:T(8,128)(2,1)S(1)} all-gather(bf16[768,64]{0,1:T(8,128)(2,1)S(1)} %convolution_convert_fusion.6), channel_id=1, replica_groups=mesh['grp'=4,'tp'=8] {'tp'}, dimensions={1}, use_global_device_ids=true | all-gather | bytes 884736 | tf_op jit(solution)/shard_map/all_gather | solution.py:73
  59.2 0.2 reshape.71
  59.3 0.0 copy-start.5
  59.4 6.5 all_gather.29
  65.9 4.3 convolution_convert_fusion.5
  70.2 32.1 %all_gather.30 = bf16[768,512]{0,1:T(8,128)(2,1)S(1)} all-gather(bf16[768,64]{0,1:T(8,128)(2,1)S(1)} %convolution_convert_fusion.5), channel_id=1, replica_groups=mesh['grp'=4,'tp'=8] {'tp'}, dimensions={1}, use_global_device_ids=true | all-gather | bytes 884736 | tf_op jit(solution)/shard_map/all_gather | solution.py:72
  102.3 0.2 reshape.72
  102.4 0.8 constant_dynamic-slice_fusion
  103.3 0.4 copy.29
  103.7 0.2 reduce_window_sum.23
  103.9 0.4 copy.41
  104.3 0.1 convert_reduce_fusion
  104.4 0.2 broadcast_compare_fusion
  104.6 0.0 all-gather.6.cloned.1.call-done
  104.6 4.7 convolution_convert_fusion.4
  109.3 0.1 reshape.73
  109.5 2.4 fusion.32
  111.8 2.1 fusion.9
  113.9 0.4 copy.33
  114.3 0.0 all-gather.8.cloned.1.call-done
  114.4 5.5 convolution_convert_fusion.1
  119.9 0.0 all-reduce.2.cloned.1.call-update
  119.9 0.0 all-gather.10.cloned.1.call-start
  119.9 0.5 all-gather.10.cloned.1.call-update
  120.5 0.0 all-gather.12.cloned.1.call-start
  120.5 0.5 all-gather.12.cloned.1.call-update
  121.1 0.2 all-gather.14.cloned.1.call-start
  121.3 0.3 all-gather.14.cloned.1.call-update
  121.6 0.0 copy-start.7
  121.7 0.0 reduce-scatter.5.cloned.1.call-start
  121.7 189.5 %all-reduce.2.cloned.1.call-done = bf16[768,3584]{1,0:T(8,128)(2,1)} async-done(((bf16[768,3584]{1,0:T(8,128)(2,1)}), bf16[768,3584]{1,0:T(8,128)(2,1)}) %all-reduce.2.cloned.1.call-update) | async-done | bytes 5505040 | tf_op jit(solution)/shard_map/psum | solution.py:101
  311.2 11.4 %convert_add_fusion = (f32[768,3584]{1,0:T(8,128)}, f32[768]{0:T(1024)S(1)}) fusion(bf16[768,3584]{1,0:T(8,128)(2,1)} %param.12, bf16[768,3584]{1,0:T(8,128)(2,1)} %all-reduce.2.cloned.1.call-done), kind=kLoop, calls=%fused_computation.1 | loop fusion | flops 13761792 | bytes 22023168 | tf_op jit(solution)/shard_map/add | solution.py:102
  322.6 51.9 %all-gather.10.cloned.1.call-done = bf16[3584,1280]{1,0:T(8,128)(2,1)} async-done(((bf16[896,1280]{1,0:T(8,128)(2,1)}), bf16[3584,1280]{1,0:T(8,128)(2,1)}) %all-gather.10.cloned.1.call-update) | async-done | bytes 9175056 | tf_op jit(solution)/shard_map/all_gather | solution.py:64
  374.5 14.7 %fusion.31 = f32[768,1280]{1,0:T(8,128)} fusion(bf16[3584,1280]{1,0:T(8,128)(2,1)} %all-gather.10.cloned.1.call-done, f32[3584]{0:T(1024)S(1)} %copy-done.7, f32[768]{0:T(1024)S(1)} %add_rsqrt_fusion, bf16[768,3584]{1,0:T(8,128)(2,1)} %param.12, bf16[768,3584]{1,0:T(8,128)(2,1)} %all-reduce.2.cloned.1.call-done), kind=kOutput, calls=%fused_computation.57 | convolution fusion | flops 7062945792 | bytes 24134656 | tf_op jit(solution)/shard_map/dot_general | solution.py:104
  389.1 49.6 %all-gather.12.cloned.1.call-done = bf16[3584,1280]{1,0:T(8,128)(2,1)} async-done(((bf16[896,1280]{1,0:T(8,128)(2,1)}), bf16[3584,1280]{1,0:T(8,128)(2,1)}) %all-gather.12.cloned.1.call-update) | async-done | bytes 9175056 | tf_op jit(solution)/shard_map/all_gather | solution.py:65
  438.7 64.3 %all-gather.14.cloned.1.call-done = bf16[3584,1280]{1,0:T(8,128)(2,1)} async-done(((bf16[896,1280]{1,0:T(8,128)(2,1)}), bf16[3584,1280]{1,0:T(8,128)(2,1)}) %all-gather.14.cloned.1.call-update) | async-done | bytes 9175056 | tf_op jit(solution)/shard_map/all_gather | solution.py:66
  503.0 25.9 %convolution_convert_fusion = bf16[768,3584]{1,0:T(8,128)(2,1)} fusion(bf16[3584,1280]{1,0:T(8,128)(2,1)} %all-gather.14.cloned.1.call-done, bf16[3584,1280]{1,0:T(8,128)(2,1)} %all-gather.12.cloned.1.call-done, f32[768,1280]{1,0:T(8,128)} %fusion.31, f32[3584]{0:T(1024)S(1)} %copy-done.7, f32[768]{0:T(1024)S(1)} %add_rsqrt_fusion, ...), kind=kOutput, calls=%fused_computation.9 | convolution fusion | flops 14118027264 | bytes 38814720 | tf_op jit(solution)/shard_map/dot_general | solution.py:32
  528.9 0.0 reduce-scatter.5.cloned.1.call-update
  529.0 0.0 reduce-scatter.7.cloned.1.call-start
  529.0 0.1 broadcast_add_fusion
  529.1 0.5 copy-done.6
  529.6 0.1 fusion.22
  529.7 0.1 dynamic-slice
  529.8 105.6 %reduce-scatter.5.cloned.1.call-done = bf16[96,3584]{1,0:T(8,128)(2,1)} async-done(((bf16[768,3584]{1,0:T(8,128)(2,1)}), bf16[96,3584]{1,0:T(8,128)(2,1)}) %reduce-scatter.5.cloned.1.call-update) | async-done | bytes 688144 | tf_op jit(solution)/shard_map/reduce_scatter | solution.py:117
  635.4 2.2 convolution_convert_fusion.2
  637.6 1.2 copy.39
  638.8 0.0 reduce-scatter.7.cloned.1.call-update
  638.8 0.2 select_reduce_fusion
  639.0 0.1 convert_element_type.92
  639.1 62.5 %reduce-scatter.7.cloned.1.call-done = bf16[448,16]{1,0:T(8,128)(2,1)} async-done(((bf16[3584,16]{1,0:T(8,128)(2,1)}), bf16[448,16]{1,0:T(8,128)(2,1)}) %reduce-scatter.7.cloned.1.call-update) | async-done | bytes 14352
  701.6 1.0 copy.40
  702.6 0.2 convolution_convert_fusion.7
  702.8 6.4 all_to_all.5
  709.2 0.6 copy.59
  (20 shorter events, 0.1 us)
Async XLA Ops:
  6.5 5.4 copy-start.2
  6.5 13.7 %copy-start.4 = (f32[3584]{0:T(1024)S(1)}, f32[3584]{0:T(1024)}, u32[]{:S(2)}) copy-start(f32[3584]{0:T(1024)} %param.15) | copy-start | bytes 43012
  6.5 98.1 %all-gather.6.cloned.1.call-start = ((), (), s32[]{:S(2)}) async-start(), calls=%async_computation.3 | async-start | bytes 2293760 | tf_op jit(solution)/shard_map/all_gather | solution.py:60
  7.3 107.1 %all-gather.8.cloned.1.call-start = ((), (), s32[]{:S(2)}) async-start(), calls=%async_computation.4 | async-start | bytes 2293760 | tf_op jit(solution)/shard_map/all_gather | solution.py:63
  8.0 303.2 %all-reduce.2.cloned.1.call-start = ((), (), s32[]{:S(2)}) async-start(), calls=%async_computation.5 | async-start | bytes 11010048 | tf_op jit(solution)/shard_map/psum | solution.py:101
  8.1 12.2 %copy-start = (bf16[768,3584]{1,0:T(8,128)(2,1)S(1)}, bf16[768,3584]{1,0:T(8,128)(2,1)}, u32[]{:S(2)}) copy-start(bf16[768,3584]{1,0:T(8,128)(2,1)} %param.12) | copy-start | bytes 16515076
  22.4 2.4 copy-start.1
  24.8 34.5 %copy-start.3 = (bf16[896,64]{0,1:T(8,128)(2,1)S(1)}, bf16[896,64]{0,1:T(8,128)(2,1)}, u32[]{:S(2)}) copy-start(bf16[896,64]{0,1:T(8,128)(2,1)} %param.17) | copy-start | bytes 344068
  59.3 44.3 %copy-start.5 = (s32[2,8]{1,0:T(2,128)S(1)}, s32[2,8]{1,0:T(2,128)}, u32[]{:S(2)}) copy-start(s32[2,8]{1,0:T(2,128)} %param.13) | copy-start | bytes 196
  119.9 254.6 %all-gather.10.cloned.1.call-start = ((), (), s32[]{:S(2)}) async-start(), calls=%async_computation.6 | async-start | bytes 11468800 | tf_op jit(solution)/shard_map/all_gather | solution.py:64
  120.5 318.2 %all-gather.12.cloned.1.call-start = ((), (), s32[]{:S(2)}) async-start(), calls=%async_computation.7 | async-start | bytes 11468800 | tf_op jit(solution)/shard_map/all_gather | solution.py:65
  121.1 381.9 %all-gather.14.cloned.1.call-start = ((), (), s32[]{:S(2)}) async-start(), calls=%async_computation.8 | async-start | bytes 11468800 | tf_op jit(solution)/shard_map/all_gather | solution.py:66
  121.6 252.8 %copy-start.7 = (f32[3584]{0:T(1024)S(1)}, f32[3584]{0:T(1024)}, u32[]{:S(2)}) copy-start(f32[3584]{0:T(1024)} %param.20) | copy-start | bytes 43012
  121.7 513.7 %reduce-scatter.5.cloned.1.call-start = ((), (), s32[]{:S(2)}) async-start(), calls=%async_computation.9 | async-start | bytes 6193152 | tf_op jit(solution)/shard_map/reduce_scatter | solution.py:117
  528.9 0.7 copy-start.6
  529.0 172.7 %reduce-scatter.7.cloned.1.call-start = ((), (), s32[]{:S(2)}) async-start(), calls=%async_computation.10 | async-start | bytes 1032192
Sparse Core Ops, SparseCore 0:
  8.9 23.8 all-gather.5
  34.3 21.1 all-gather.7
  120.0 191.1 all-reduce.1
  312.7 61.7 all-gather.9
  375.9 62.7 all-gather.11
  440.2 62.7 all-gather.13
  529.1 106.2 reduce-scatter.4
  639.0 62.6 reduce-scatter.6
where the time goes:
time: 717 us
  waiting for transfers between devices  526 us (73%)
  blocking collectives  85.8 us (12%)
  matrix products  63.7 us (9%)
  other arithmetic  18.3 us (3%)
  between operations  13.7 us (2%)
  local copies, waits for them, and re-layouts  8.39 us (1%)
    psum x1, waiting for transfers between devices, on_device(): lax.psum(attn_term.astype(jnp.bfloat16), 'tp').astype(jnp.float32)  189 us
    reduce_scatter x1, waiting for transfers between devices, on_device(): lax.psum_scatter(ffn_term.astype(jnp.bfloat16), 'tp', scatter_dimension=0...  106 us
    unnamed x9, waiting for transfers between devices  65.4 us
    all_gather x1, waiting for transfers between devices, on_device(): lax.all_gather(down_weight, 'grp', axis=0, tiled=True)  64.3 us
    all_gather x1, waiting for transfers between devices, on_device(): lax.all_gather(gate_weight, 'grp', axis=0, tiled=True)  51.9 us
    all_gather x1, waiting for transfers between devices, on_device(): lax.all_gather(up_weight, 'grp', axis=0, tiled=True)  49.6 us
    all_gather x1, blocking collectives, on_device(): lax.all_gather(value_part, 'tp', axis=1, tiled=True)  32.6 us
    all_gather x1, blocking collectives, on_device(): lax.all_gather(key_part, 'tp', axis=1, tiled=True)  32.1 us
  transfers between devices with their start and end apart: 8, of which 6 were waited for; matrix products, arithmetic and copies ran while one was open for 7% of the time, Pallas kernels for 0%

commit v1 on v0

--- a/solution.py
+++ b/solution.py
@@ -8,6 +8,28 @@
 HEADS = 16
 EPSILON = 1e-06
 HIGH = lax.Precision.HIGHEST
+
+
+def in_order(tiles, dim):
+    tiles = jnp.moveaxis(tiles, 0, dim)
+    shape = tiles.shape
+    return tiles.reshape(*shape[:dim], shape[dim] * shape[dim + 1], *shape[dim + 2 :])
+
+
+def collected_by_bits(shard, axis):
+    peers = lax.axis_size(axis)
+    tiles = shard[None]
+    for level in range(peers.bit_length() - 1):
+        bit = 1 << level
+        other = lax.ppermute(tiles, axis, [(i, i ^ bit) for i in range(peers)])
+        both = jnp.stack([tiles, other])
+        upper = lax.axis_index(axis) >> level & 1
+        tiles = jnp.where(upper == 0, both, both[::-1]).reshape(-1, *shard.shape)
+    return tiles
+
+
+def gather_by_bits(x, axis, dim):
+    return in_order(collected_by_bits(x, axis), dim)
 
 
 def rms_scale(rows, gain):
@@ -61,7 +83,7 @@
         lax.all_gather(k_weight, "grp", axis=0, tiled=True),
         lax.all_gather(v_weight, "grp", axis=0, tiled=True),
         lax.all_gather(o_weight, "grp", axis=0, tiled=True),
-        lax.all_gather(gate_weight, "grp", axis=0, tiled=True),
+        gather_by_bits(gate_weight, "grp", 0),
         lax.all_gather(up_weight, "grp", axis=0, tiled=True),
         lax.all_gather(down_weight, "grp", axis=0, tiled=True),
     )

time: 717 us -> 653 us (0.911)
  waiting for transfers between devices: 526 us -> 433 us
  other arithmetic: 18.3 us -> 46.8 us
    psum x1, waiting for transfers between devices: 189 us -> 55.4 us  [on_device(): lax.psum(attn_term.astype(jnp.bfloat16), 'tp').astype(jnp.float32)]
    ppermute x0 -> x2, waiting for transfers between devices: none -> 105 us  [collected_by_bits(): other = lax.ppermute(tiles, axis, [(i, i ^ bit) for i in range(peers)])]
    all_gather x1 -> x0, waiting for transfers between devices: 51.9 us -> none  [on_device(): lax.all_gather(gate_weight, 'grp', axis=0, tiled=True)]
    all_gather x1, waiting for transfers between devices: 64.3 us -> 38.7 us  [on_device(): lax.all_gather(down_weight, 'grp', axis=0, tiled=True)]
    another operation x0 -> x3, other arithmetic: none -> 15.1 us  [collected_by_bits(): both = jnp.stack([tiles, other])]
    all_gather x1, waiting for transfers between devices: 49.6 us -> 64.3 us  [on_device(): lax.all_gather(up_weight, 'grp', axis=0, tiled=True)]
    select_n x0 -> x1, other arithmetic: none -> 13.2 us  [collected_by_bits(): tiles = jnp.where(upper == 0, both, both[::-1]).reshape(-1, *shard.shape)]
    unnamed x9 -> x8, waiting for transfers between devices: 65.4 us -> 64.9 us
  transfers between devices with their start and end apart: 8 -> 9, of which waited for: 6 -> 7; matrix products, arithmetic and copies ran while one was open for 7% -> 12% of each run, Pallas kernels for 0% -> 0%
where the time goes in v1:
time: 653 us
  waiting for transfers between devices  433 us (66%)
  blocking collectives  85.8 us (13%)
  matrix products  62 us (9%)
  other arithmetic  46.8 us (7%)
  between operations  13.7 us (2%)
  local copies, waits for them, and re-layouts  9.52 us (1%)
    reduce_scatter x1, waiting for transfers between devices, on_device(): lax.psum_scatter(ffn_term.astype(jnp.bfloat16), 'tp', scatter_dimension=0...  106 us
    ppermute x2, waiting for transfers between devices, collected_by_bits(): other = lax.ppermute(tiles, axis, [(i, i ^ bit) for i in range(peers)])  105 us
    unnamed x8, waiting for transfers between devices  64.9 us
    all_gather x1, waiting for transfers between devices, on_device(): lax.all_gather(up_weight, 'grp', axis=0, tiled=True)  64.3 us
    psum x1, waiting for transfers between devices, on_device(): lax.psum(attn_term.astype(jnp.bfloat16), 'tp').astype(jnp.float32)  55.4 us
    all_gather x1, waiting for transfers between devices, on_device(): lax.all_gather(down_weight, 'grp', axis=0, tiled=True)  38.7 us
    all_gather x1, blocking collectives, on_device(): lax.all_gather(value_part, 'tp', axis=1, tiled=True)  32.6 us
    all_gather x1, blocking collectives, on_device(): lax.all_gather(key_part, 'tp', axis=1, tiled=True)  32.1 us
  transfers between devices with their start and end apart: 9, of which 7 were waited for; matrix products, arithmetic and copies ran while one was open for 12% of the time, Pallas kernels for 0%

profile of v1, /device:TPU:0, one launch (start us, length us, event | category | flops | bytes accessed | tf_op | source)
XLA Modules:
  0.0 653.0 jit_solution(9011654634883844832)
XLA Ops:
  6.5 0.7 all-gather.5.cloned.1.call-update
  7.3 0.0 all-gather.7.cloned.1.call-start
  7.3 0.7 all-gather.7.cloned.1.call-update
  8.0 0.0 all-reduce.2.cloned.1.call-start
  8.1 3.9 fusion.1
  11.9 8.3 %all_gather.24 = bf16[3584,64]{0,1:T(8,128)(2,1)S(1)} all-gather(bf16[896,64]{0,1:T(8,128)(2,1)S(1)} %copy-done.4), channel_id=1, replica_groups=mesh['grp'=4,'tp'=8] {'grp'}, dimensions={0}, use_global_device_ids=true | all-gather | bytes 573440 | tf_op jit(solution)/shard_map/all_gather | solution.py:84
  20.2 2.2 fusion.3
  22.4 2.4 copy-done.1
  24.8 1.8 convolution_convert_fusion.6
  26.6 32.6 %all_gather.25 = bf16[768,512]{0,1:T(8,128)(2,1)S(1)} all-gather(bf16[768,64]{0,1:T(8,128)(2,1)S(1)} %convolution_convert_fusion.6), channel_id=1, replica_groups=mesh['grp'=4,'tp'=8] {'tp'}, dimensions={1}, use_global_device_ids=true | all-gather | bytes 884736 | tf_op jit(solution)/shard_map/all_gather | solution.py:95
  59.2 0.2 reshape.74
  59.4 6.5 all_gather.26
  65.9 4.3 convolution_convert_fusion.5
  70.2 32.1 %all_gather.27 = bf16[768,512]{0,1:T(8,128)(2,1)S(1)} all-gather(bf16[768,64]{0,1:T(8,128)(2,1)S(1)} %convolution_convert_fusion.5), channel_id=1, replica_groups=mesh['grp'=4,'tp'=8] {'tp'}, dimensions={1}, use_global_device_ids=true | all-gather | bytes 884736 | tf_op jit(solution)/shard_map/all_gather | solution.py:94
  102.3 0.2 reshape.75
  102.5 0.8 constant_dynamic-slice_fusion
  103.3 0.4 copy.29
  103.7 0.2 reduce_window_sum.23
  103.9 0.4 copy.41
  104.3 0.1 convert_reduce_fusion
  104.4 0.6 copy-done.6
  105.0 0.2 broadcast_compare_fusion
  105.2 0.0 all-gather.5.cloned.1.call-done
  105.2 4.7 convolution_convert_fusion.4
  109.9 0.1 reshape.76
  110.0 2.3 fusion.34
  112.4 2.1 fusion.11
  114.4 0.4 copy.33
  114.9 0.0 all-gather.7.cloned.1.call-done
  114.9 5.5 convolution_convert_fusion.1
  120.4 0.0 all-gather.11.cloned.1.call-start
  120.5 0.5 all-gather.11.cloned.1.call-update
  121.0 0.2 all-gather.9.cloned.1.call-start
  121.2 0.4 all-gather.9.cloned.1.call-update
  121.6 0.0 reduce-scatter.5.cloned.1.call-start
  121.6 0.4 copy-done.3
  122.1 4.6 collective-permute-done
  126.6 2.4 pad_maximum_fusion.1
  129.0 4.5 fusion.5
  133.5 1.4 collective-permute-start.1
  134.9 100.1 %collective-permute-done.1 = bf16[2,896,1280]{2,1,0:T(8,128)(2,1)} collective-permute-done((bf16[2,896,1280]{2,1,0:T(8,128)(2,1)}, bf16[2,896,1280]{2,1,0:T(8,128)(2,1)}, u32[]{:S(2)}, u32[]{:S(2)}) %collective-permute-start.1) | collective-permute-done | bytes 4587552 | tf_op jit(solution)/shard_map/ppermute | solution.py:24
  235.0 8.2 %pad_maximum_fusion = bf16[2,2,896,1280]{3,2,1,0:T(8,128)(2,1)} fusion(bf16[1,2,896,1280]{3,2,1,0:T(8,128)(2,1)} %bitcast.13, bf16[1,2,896,1280]{3,2,1,0:T(8,128)(2,1)} %get-tuple-element.7), kind=kLoop, calls=%fused_computation.10 | loop fusion | flops 4587520 | bytes 18350080 | tf_op jit(solution)/shard_map/stack | solution.py:25
  243.2 13.2 %reverse_select_fusion = bf16[2,2,896,1280]{3,2,1,0:T(8,128)(2,1)} fusion(bf16[2,2,896,1280]{3,2,1,0:T(8,128)(2,1)} %pad_maximum_fusion, pred[]{:T(512)S(6)} %eq.56), kind=kLoop, calls=%fused_computation.4 | loop fusion | flops 4587520 | bytes 18350080 | tf_op jit(solution)/shard_map/jit(_where)/select_n | solution.py:27
  256.4 55.4 %all-reduce.2.cloned.1.call-done = bf16[768,3584]{1,0:T(8,128)(2,1)} async-done(((bf16[768,3584]{1,0:T(8,128)(2,1)}), bf16[768,3584]{1,0:T(8,128)(2,1)}) %all-reduce.2.cloned.1.call-update) | async-done | bytes 5505040 | tf_op jit(solution)/shard_map/psum | solution.py:123
  311.7 11.6 %convert_add_fusion = (f32[768,3584]{1,0:T(8,128)}, f32[768]{0:T(1024)S(1)}) fusion(bf16[768,3584]{1,0:T(8,128)(2,1)} %param.12, bf16[768,3584]{1,0:T(8,128)(2,1)} %all-reduce.2.cloned.1.call-done), kind=kLoop, calls=%fused_computation.1 | loop fusion | flops 13761792 | bytes 22023168 | tf_op jit(solution)/shard_map/add | solution.py:124
  323.3 13.0 %fusion.33 = f32[768,1280]{1,0:T(8,128)} fusion(bf16[3584,1280]{1,0:T(8,128)(2,1)S(1)} %bitcast.54, f32[3584]{0:T(1024)S(1)} %copy-done.12, f32[768]{0:T(1024)S(1)} %add_rsqrt_fusion, bf16[768,3584]{1,0:T(8,128)(2,1)} %param.12, bf16[768,3584]{1,0:T(8,128)(2,1)} %all-reduce.2.cloned.1.call-done), kind=kOutput, calls=%fused_computation.63 | convolution fusion | flops 7062945792 | bytes 24134656 | tf_op jit(solution)/shard_map/dot_general | solution.py:126
  336.3 38.7 %all-gather.11.cloned.1.call-done = bf16[3584,1280]{1,0:T(8,128)(2,1)} async-done(((bf16[896,1280]{1,0:T(8,128)(2,1)}), bf16[3584,1280]{1,0:T(8,128)(2,1)}) %all-gather.11.cloned.1.call-update) | async-done | bytes 9175056 | tf_op jit(solution)/shard_map/all_gather | solution.py:88
  375.0 64.3 %all-gather.9.cloned.1.call-done = bf16[3584,1280]{1,0:T(8,128)(2,1)} async-done(((bf16[896,1280]{1,0:T(8,128)(2,1)}), bf16[3584,1280]{1,0:T(8,128)(2,1)}) %all-gather.9.cloned.1.call-update) | async-done | bytes 9175056 | tf_op jit(solution)/shard_map/all_gather | solution.py:87
  439.3 25.9 %convolution_convert_fusion = bf16[768,3584]{1,0:T(8,128)(2,1)} fusion(bf16[3584,1280]{1,0:T(8,128)(2,1)} %all-gather.11.cloned.1.call-done, bf16[3584,1280]{1,0:T(8,128)(2,1)} %all-gather.9.cloned.1.call-done, f32[768,1280]{1,0:T(8,128)} %fusion.33, f32[3584]{0:T(1024)S(1)} %copy-done.12, f32[768]{0:T(1024)S(1)} %add_rsqrt_fusion, ...), kind=kOutput, calls=%fused_computation.12 | convolution fusion | flops 14118027264 | bytes 38814720 | tf_op jit(solution)/shard_map/dot_general | solution.py:54
  465.2 0.0 reduce-scatter.7.cloned.1.call-start
  465.3 0.6 copy-done.7
  465.9 0.1 broadcast_add_fusion
  466.0 0.1 fusion.24
  466.1 0.1 dynamic-slice
  466.1 105.5 %reduce-scatter.5.cloned.1.call-done = bf16[96,3584]{1,0:T(8,128)(2,1)} async-done(((bf16[768,3584]{1,0:T(8,128)(2,1)}), bf16[96,3584]{1,0:T(8,128)(2,1)}) %reduce-scatter.5.cloned.1.call-update) | async-done | bytes 688144 | tf_op jit(solution)/shard_map/reduce_scatter | solution.py:139
  571.7 2.2 convolution_convert_fusion.2
  573.9 1.3 copy.39
  575.1 0.2 select_reduce_fusion
  575.3 0.1 convert_element_type.92
  575.4 62.5 %reduce-scatter.7.cloned.1.call-done = bf16[448,16]{1,0:T(8,128)(2,1)} async-done(((bf16[3584,16]{1,0:T(8,128)(2,1)}), bf16[448,16]{1,0:T(8,128)(2,1)}) %reduce-scatter.7.cloned.1.call-update) | async-done | bytes 14352
  638.0 1.0 copy.40
  638.9 0.2 convolution_convert_fusion.7
  639.1 6.4 all_to_all.5
  645.6 0.6 copy.59
  (35 shorter events, 0.2 us)
Async XLA Ops:
  6.5 5.4 copy-start.4
  6.5 13.7 %copy-start.8 = (f32[3584]{0:T(1024)S(1)}, f32[3584]{0:T(1024)}, u32[]{:S(2)}) copy-start(f32[3584]{0:T(1024)} %param.15) | copy-start | bytes 43012
  6.5 98.7 %all-gather.5.cloned.1.call-start = ((), (), s32[]{:S(2)}) async-start(), calls=%async_computation.3 | async-start | bytes 2293760 | tf_op jit(solution)/shard_map/all_gather | solution.py:82
  7.3 107.6 %all-gather.7.cloned.1.call-start = ((), (), s32[]{:S(2)}) async-start(), calls=%async_computation.4 | async-start | bytes 2293760 | tf_op jit(solution)/shard_map/all_gather | solution.py:85
  8.0 303.7 %all-reduce.2.cloned.1.call-start = ((), (), s32[]{:S(2)}) async-start(), calls=%async_computation.5 | async-start | bytes 11010048 | tf_op jit(solution)/shard_map/psum | solution.py:123
  8.1 12.2 %copy-start = (bf16[768,3584]{1,0:T(8,128)(2,1)S(1)}, bf16[768,3584]{1,0:T(8,128)(2,1)}, u32[]{:S(2)}) copy-start(bf16[768,3584]{1,0:T(8,128)(2,1)} %param.12) | copy-start | bytes 16515076
  22.4 2.4 copy-start.1
  24.8 34.5 %copy-start.5 = (bf16[896,64]{0,1:T(8,128)(2,1)S(1)}, bf16[896,64]{0,1:T(8,128)(2,1)}, u32[]{:S(2)}) copy-start(bf16[896,64]{0,1:T(8,128)(2,1)} %param.17) | copy-start | bytes 344068
  59.4 44.3 %copy-start.9 = (s32[2,8]{1,0:T(2,128)S(1)}, s32[2,8]{1,0:T(2,128)}, u32[]{:S(2)}) copy-start(s32[2,8]{1,0:T(2,128)} %param.13) | copy-start | bytes 196
  104.4 0.6 copy-start.6
  120.4 1.6 copy-start.3
  120.4 254.6 %all-gather.11.cloned.1.call-start = ((), (), s32[]{:S(2)}) async-start(), calls=%async_computation.7 | async-start | bytes 11468800 | tf_op jit(solution)/shard_map/all_gather | solution.py:88
  121.0 318.3 %all-gather.9.cloned.1.call-start = ((), (), s32[]{:S(2)}) async-start(), calls=%async_computation.6 | async-start | bytes 11468800 | tf_op jit(solution)/shard_map/all_gather | solution.py:87
  121.6 450.1 %reduce-scatter.5.cloned.1.call-start = ((), (), s32[]{:S(2)}) async-start(), calls=%async_computation.8 | async-start | bytes 6193152 | tf_op jit(solution)/shard_map/reduce_scatter | solution.py:139
  122.0 4.6 collective-permute-start
  133.5 101.5 %collective-permute-start.1 = (bf16[2,896,1280]{2,1,0:T(8,128)(2,1)}, bf16[2,896,1280]{2,1,0:T(8,128)(2,1)}, u32[]{:S(2)}, u32[]{:S(2)}) collective-permute-start(bf16[2,896,1280]{2,1,0:T(8,128)(2,1)} %get-tuple-element.8), channel_id=1, source_target_pairs={{0,16},{8,24},{16,0},{24,8},{1,17},{9,25},{17,1},{25,9},{2,18},{10... | collective-permute-start | bytes 13762568 | tf_op jit(solution)/shard_map/ppermute | solution.py:24
  256.4 67.0 %copy-start.12 = (f32[3584]{0:T(1024)S(1)}, f32[3584]{0:T(1024)}, u32[]{:S(2)}) copy-start(f32[3584]{0:T(1024)} %param.20) | copy-start | bytes 43012
  311.7 11.6 %copy-start.2 = (bf16[2,2,896,1280]{3,2,1,0:T(8,128)(2,1)S(1)}, bf16[2,2,896,1280]{3,2,1,0:T(8,128)(2,1)}, u32[]{:S(2)}) copy-start(bf16[2,2,896,1280]{3,2,1,0:T(8,128)(2,1)} %reverse_select_fusion) | copy-start | bytes 27525124
  465.2 0.7 copy-start.7
  465.2 0.8 copy-start.11
  465.2 110.1 %copy-start.10 = (s32[2,8]{1,0:T(2,128)S(1)}, s32[2,8]{1,0:T(2,128)}, u32[]{:S(2)}) copy-start(s32[2,8]{1,0:T(2,128)} %param.13) | copy-start | bytes 196
  465.2 172.7 %reduce-scatter.7.cloned.1.call-start = ((), (), s32[]{:S(2)}) async-start(), calls=%async_computation.9 | async-start | bytes 1032192
Sparse Core Ops, SparseCore 0:
  8.9 23.8 all-gather.4
  34.3 21.1 all-gather.6
  120.5 191.1 all-reduce.1
  313.2 61.7 all-gather.10
  376.5 62.7 all-gather.8
  465.4 106.2 reduce-scatter.4
  575.3 62.6 reduce-scatter.6
